TPU v7x, 512 devices: a whole 4x4x16 slice. The times are simulated.
512 devices in a mesh: dp: 64 (over z, x), pair: 8 (over y, core).
Axes of the slice: x: 4, y: 4, z: 16, core: 2. Of those that a mesh axis runs over, the one named last changes fastest.
Arguments:
- embedding: bfloat16 [65536, 1024], P(('dp', 'pair')), may hold values from -32 to 32
- labels: int32 [65536], P(('dp', 'pair')), may hold values from 0 to 127, as said below
- order_ids: int32 [65536], P(('dp', 'pair')), may hold values from 0 to 65535, each once
Outputs:
- best_similarity: float32 [65536], P(('dp', 'pair'))
Inputs may be any that keep to these rules, and one draw needn't show every extreme that they name: `labels`: clusters 2 * g to 2 * g + 1 form owner group g. Among the 128 rows of one device (aligned blocks of the whole array) at most 4 name clusters of any one group, and in every draw some group gets exactly 4 rows from every device.
All inputs are finite; a program needn't handle non-finite values.
Results may differ from a plain program's by a relative error of at most 0.00049.
Values may be sent and summed in bfloat16 or wider, within the bound.
No kernel may reach another device: no remote copies, remote signals or barrier semaphores. Data moves between devices by JAX's collectives and lax.ppermute only.
A program may use at most 64 MiB of HBM per device.

v0:
```python
import jax
import jax.numpy as jnp
from jax import lax
from jax.sharding import PartitionSpec as P

CL_OWN = 2


def tile_best(own_rows, own_labels, own_order, other_rows, other_labels, other_order):
    scores = jnp.dot(own_rows, other_rows.T, preferred_element_type=jnp.float32)
    same_cluster = (other_labels[None, :] == own_labels[:, None]) & (own_labels[:, None] >= 0)
    earlier = same_cluster & (other_order[None, :] < own_order[:, None])
    after_own = same_cluster & (own_order[:, None] < other_order[None, :])
    ahead = jnp.max(jnp.where(earlier, scores, -1.0), axis=1)
    behind = jnp.max(jnp.where(after_own, scores, -1.0), axis=0)
    return (ahead, behind)


def on_device(embedding, labels, order_ids):
    groups = lax.axis_size("dp")
    rows_here = embedding.shape[0]
    capacity = 2 * rows_here // groups
    slot_count = groups * capacity
    values = embedding.astype(jnp.float32)
    squares = jnp.sum(values * values, axis=1, keepdims=True)
    shifted = squares + 1e-06
    unit_rows = (values * lax.rsqrt(shifted)).astype(jnp.bfloat16)
    owner_group = labels // CL_OWN
    onehot = (owner_group[:, None] == jnp.arange(groups, dtype=jnp.int32)[None, :]).astype(
        jnp.int32
    )
    before = jnp.cumsum(onehot, axis=0) - onehot
    slot_index = owner_group * capacity + jnp.sum(before * onehot, axis=1)
    send_rows = (
        jnp.zeros((slot_count, unit_rows.shape[1]), jnp.bfloat16).at[slot_index].set(unit_rows)
    )
    send_labels = jnp.full((slot_count,), -1, jnp.int32).at[slot_index].set(labels)
    send_order = jnp.zeros((slot_count,), jnp.int32).at[slot_index].set(order_ids)
    got_rows, got_labels, got_order = (
        lax.all_to_all(
            send_rows.reshape(groups, capacity, -1), "dp", split_axis=0, concat_axis=0, tiled=True
        ),
        lax.all_to_all(
            send_labels.reshape(groups, capacity), "dp", split_axis=0, concat_axis=0, tiled=True
        ),
        lax.all_to_all(
            send_order.reshape(groups, capacity), "dp", split_axis=0, concat_axis=0, tiled=True
        ),
    )
    got_rows = got_rows.reshape(slot_count, -1)
    got_labels = got_labels.reshape(slot_count)
    got_order = got_order.reshape(slot_count)
    best_seen = jnp.full((slot_count,), -1.0, jnp.float32)
    piece = (
        lax.all_gather(got_rows, "pair", axis=0, tiled=True),
        lax.all_gather(got_labels, "pair", axis=0, tiled=True),
        lax.all_gather(got_order, "pair", axis=0, tiled=True),
    )
    piece_count = piece[0].shape[0]
    for offset in range(0, piece_count, 512):
        width_now = min(512, piece_count - offset)
        found = tile_best(
            got_rows,
            got_labels,
            got_order,
            piece[0][offset : offset + width_now],
            piece[1][offset : offset + width_now],
            piece[2][offset : offset + width_now],
        )
        best_seen = jnp.maximum(best_seen, found[0])
    answered = lax.all_to_all(
        best_seen.reshape(groups, capacity), "dp", split_axis=0, concat_axis=0, tiled=True
    )
    return answered.reshape(slot_count)[slot_index]


def solution(mesh):
    in_specs = (P(("dp", "pair"), None), P(("dp", "pair")), P(("dp", "pair")))
    out_specs = P(("dp", "pair"))
    return jax.shard_map(
        on_device, mesh=mesh, in_specs=in_specs, out_specs=out_specs, check_vma=False
    )
```

profile of v0, /device:TPU:8, one launch (start us, length us, event | category | flops | bytes accessed | tf_op | source)
XLA Modules:
  0.0 161.8 jit_solution(7379392571141710078)
XLA Ops:
  6.5 0.7 and_select_fusion
  7.2 1.1 fusion.8
  8.4 0.2 reduce_window_sum.11
  8.6 0.2 select_reduce_fusion
  8.7 0.7 compare_select_fusion
  9.4 1.8 %scatter_custom_fusion.2 = bf16[256,1024]{1,0:T(8,128)(2,1)S(1)} fusion(s32[128]{0:T(128)S(1)} %compare_select_fusion, bf16[128,1024]{1,0:T(8,128)(2,1)} %param.3, f32[128]{0:T(128)S(1)} %add_rsqrt_fusion, bf16[]{:T(256)} %constant.18.clone.1), kind=kCustom, calls=%fused_computation.20 | custom fusion | flops 393216 | bytes 786946 | tf_op jit(solution)/shard_map/scatter | solution.py:35
  11.2 0.2 reshape.107
  11.4 51.2 %all_to_all.29 = bf16[64,4,1024]{2,1,0:T(4,128)(2,1)S(1)} all-to-all(bf16[64,4,1024]{2,1,0:T(4,128)(2,1)S(1)} %reshape.107), channel_id=1, replica_groups=mesh['dp'=64,'pair'=8] {'dp'}, dimensions={0} | all-to-all | bytes 1048576 | tf_op jit(solution)/shard_map/all_to_all | solution.py:40
  62.6 0.9 reshape.108
  63.5 1.2 scatter_custom_fusion
  64.8 0.7 all_to_all.19
  65.5 5.8 %all-to-all-start = ((s32[64,1,4]{2,1,0:T(1,128)}), s32[64,1,4]{2,1,0:T(1,128)S(1)}, u32[]{:S(2)}, u32[]{:S(2)}) async-start(s32[64,1,4]{2,1,0:T(1,128)} %bitcast), calls=%async_computation | async-start | bytes 65536 | tf_op jit(solution)/shard_map/all_to_all | solution.py:43
  71.3 1.1 scatter_custom_fusion.1
  72.4 0.7 all_to_all.21
  73.2 12.9 %all-to-all-done = s32[64,1,4]{2,1,0:T(1,128)S(1)} async-done(((s32[64,1,4]{2,1,0:T(1,128)}), s32[64,1,4]{2,1,0:T(1,128)S(1)}, u32[]{:S(2)}, u32[]{:S(2)}) %all-to-all-start) | async-done | bytes 1056 | tf_op jit(solution)/shard_map/all_to_all | solution.py:43
  86.1 4.5 %all-to-all-start.1 = ((s32[64,1,4]{2,1,0:T(1,128)}), s32[64,1,4]{2,1,0:T(1,128)S(1)}, u32[]{:S(2)}, u32[]{:S(2)}) async-start(s32[64,1,4]{2,1,0:T(1,128)} %bitcast.2), calls=%async_computation.1 | async-start | bytes 65536 | tf_op jit(solution)/shard_map/all_to_all | solution.py:46
  90.7 14.5 %all-to-all-done.1 = s32[64,1,4]{2,1,0:T(1,128)S(1)} async-done(((s32[64,1,4]{2,1,0:T(1,128)}), s32[64,1,4]{2,1,0:T(1,128)S(1)}, u32[]{:S(2)}, u32[]{:S(2)}) %all-to-all-start.1) | async-done | bytes 1056 | tf_op jit(solution)/shard_map/all_to_all | solution.py:46
  105.3 0.5 broadcast.74
  105.8 0.7 reduce.13
  106.7 0.7 reduce.14
  107.5 8.8 %all-gather = s32[8,1,256]{2,1,0:T(1,128)S(1)} all-gather(s32[1,1,256]{2,1,0:T(1,128)S(1)} %reshape.146), channel_id=1, replica_groups=mesh['dp'=64,'pair'=8] {'pair'}, dimensions={0}, use_global_device_ids=true | all-gather | bytes 9216 | tf_op jit(solution)/shard_map/all_gather | solution.py:56
  116.3 10.3 %all-gather.1 = s32[8,1,256]{2,1,0:T(1,128)S(1)} all-gather(s32[1,1,256]{2,1,0:T(1,128)S(1)} %reshape.148), channel_id=1, replica_groups=mesh['dp'=64,'pair'=8] {'pair'}, dimensions={0}, use_global_device_ids=true | all-gather | bytes 9216 | tf_op jit(solution)/shard_map/all_gather | solution.py:57
  126.6 2.1 %fusion.3 = f32[256]{0:T(256)S(1)} fusion(bf16[256,1024]{1,0:T(8,128)(2,1)} %reshape.108, bf16[2048,1024]{1,0:T(8,128)(2,1)} %all-gather.4.cloned.1.call-done, s32[512]{0:T(512)S(1)} %bitcast.29, s32[512]{0:T(512)S(1)} %bitcast.26, pred[256]{0:T(512)(128)(4,1)S(1)} %broadcast_compare_fusion, s32[256]{0:T(256)S(1)} %reshape.106, s32[256]{0:T(256)S(1)} %reshape.105), kind=kOutput, calls=%fused_computation.11 | convolution fusion | flops 269221632 | bytes 1580288 | tf_op jit(solution)/shard_map/dot_general | solution.py:10
  128.7 1.8 %fusion.2 = f32[256]{0:T(256)S(1)} fusion(bf16[256,1024]{1,0:T(8,128)(2,1)S(1)} %copy-done, bf16[2048,1024]{1,0:T(8,128)(2,1)} %all-gather.4.cloned.1.call-done, s32[512]{0:T(512)S(1)} %bitcast.28, s32[512]{0:T(512)S(1)} %bitcast.25, pred[256]{0:T(512)(128)(4,1)S(1)} %broadcast_compare_fusion, s32[256]{0:T(256)S(1)} %reshape.106, s32[256]{0:T(256)S(1)} %reshape.105), kind=kOutput, calls=%fused_computation.10 | convolution fusion | flops 269221632 | bytes 1580288 | tf_op jit(solution)/shard_map/dot_general | solution.py:10
  130.5 0.6 fusion.1
  131.1 0.6 fusion
  131.7 0.7 max.41
  132.4 4.6 %all-to-all-start.3 = ((f32[64,1,4]{2,1,0:T(1,128)}), f32[64,1,4]{2,1,0:T(1,128)S(1)}, u32[]{:S(2)}, u32[]{:S(2)}) async-start(f32[64,1,4]{2,1,0:T(1,128)} %bitcast.10), calls=%async_computation.3 | async-start | bytes 65536 | tf_op jit(solution)/shard_map/all_to_all | solution.py:71
  137.1 14.8 %all-to-all-done.3 = f32[64,1,4]{2,1,0:T(1,128)S(1)} async-done(((f32[64,1,4]{2,1,0:T(1,128)}), f32[64,1,4]{2,1,0:T(1,128)S(1)}, u32[]{:S(2)}, u32[]{:S(2)}) %all-to-all-start.3) | async-done | bytes 1056 | tf_op jit(solution)/shard_map/all_to_all | solution.py:71
  151.8 0.5 broadcast.76
  152.3 0.7 reduce.15
  153.2 1.8 %gather_fusion = f32[128]{0:T(128)} fusion(f32[256]{0:T(256)S(1)} %reshape.109, s32[1024]{0:T(1024)S(1)} %pad_clamp_fusion), kind=kCustom, calls=%fused_computation | custom fusion | bytes 1536 | tf_op jit(solution)/shard_map/gather | solution.py:74
  (19 shorter events, 0.7 us)
Async XLA Ops:
  6.5 120.1 %all-gather.4.cloned.1.call-start = ((), (), s32[]{:S(2)}) async-start(), calls=%async_computation.4 | async-start | bytes 4718592 | tf_op jit(solution)/shard_map/all_gather | solution.py:55
  63.5 65.2 %copy-start = (bf16[256,1024]{1,0:T(8,128)(2,1)S(1)}, bf16[256,1024]{1,0:T(8,128)(2,1)}, u32[]{:S(2)}) copy-start(bf16[256,1024]{1,0:T(8,128)(2,1)} %reshape.108) | copy-start | bytes 1572868
  65.5 20.6 %all-to-all-start = ((s32[64,1,4]{2,1,0:T(1,128)}), s32[64,1,4]{2,1,0:T(1,128)S(1)}, u32[]{:S(2)}, u32[]{:S(2)}) async-start(s32[64,1,4]{2,1,0:T(1,128)} %bitcast), calls=%async_computation | async-start | bytes 65536 | tf_op jit(solution)/shard_map/all_to_all | solution.py:43
  86.1 19.1 %all-to-all-start.1 = ((s32[64,1,4]{2,1,0:T(1,128)}), s32[64,1,4]{2,1,0:T(1,128)S(1)}, u32[]{:S(2)}, u32[]{:S(2)}) async-start(s32[64,1,4]{2,1,0:T(1,128)} %bitcast.2), calls=%async_computation.1 | async-start | bytes 65536 | tf_op jit(solution)/shard_map/all_to_all | solution.py:46
  126.6 3.9 %copy-start.1 = (bf16[2048,1024]{1,0:T(8,128)(2,1)S(1)}, bf16[2048,1024]{1,0:T(8,128)(2,1)}, u32[]{:S(2)}) copy-start(bf16[2048,1024]{1,0:T(8,128)(2,1)} %all-gather.4.cloned.1.call-done) | copy-start | bytes 12582916
  132.4 19.4 %all-to-all-start.3 = ((f32[64,1,4]{2,1,0:T(1,128)}), f32[64,1,4]{2,1,0:T(1,128)S(1)}, u32[]{:S(2)}, u32[]{:S(2)}) async-start(f32[64,1,4]{2,1,0:T(1,128)} %bitcast.10), calls=%async_computation.3 | async-start | bytes 65536 | tf_op jit(solution)/shard_map/all_to_all | solution.py:71
Sparse Core Ops, SparseCore 0:
  63.7 30.4 all-gather.3
where the time goes:
time: 162 us
  blocking collectives  70.2 us (43%)
  waiting for transfers between devices  42.3 us (26%)
  starting transfers between devices  15 us (9%)
  between operations  13.5 us (8%)
  local copies, waits for them, and re-layouts  8.9 us (5%)
  other arithmetic  6.85 us (4%)
  matrix products  5.07 us (3%)
    all_to_all x1, blocking collectives, on_device(): lax.all_to_all(send_rows.reshape(groups, capacity, -1), 'dp', split_axis=...  51.2 us
    all_to_all x1, waiting for transfers between devices, on_device(): lax.all_to_all(best_seen.reshape(groups, capacity), 'dp', split_axis=0, c...  14.8 us
    all_to_all x1, waiting for transfers between devices, on_device(): lax.all_to_all(send_order.reshape(groups, capacity), 'dp', split_axis=0,...  14.5 us
    all_to_all x1, waiting for transfers between devices, on_device(): lax.all_to_all(send_labels.reshape(groups, capacity), 'dp', split_axis=0,...  12.9 us
    all_gather x1, blocking collectives, on_device(): lax.all_gather(got_order, 'pair', axis=0, tiled=True)  10.3 us
    all_gather x1, blocking collectives, on_device(): lax.all_gather(got_labels, 'pair', axis=0, tiled=True)  8.77 us
    all_to_all x1, starting transfers between devices, on_device(): lax.all_to_all(send_labels.reshape(groups, capacity), 'dp', split_axis=0,...  5.83 us
    dot_general x4, matrix products, tile_best(): scores = jnp.dot(own_rows, other_rows.T, preferred_element_type=jnp.float32)  5.07 us
  transfers between devices with their start and end apart: 4, of which 3 were waited for; matrix products, arithmetic and copies ran while one was open for 3% of the time, Pallas kernels for 0%

commit v1 on v0

--- a/solution.py
+++ b/solution.py
@@ -17,6 +17,13 @@
 
 
 def on_device(embedding, labels, order_ids):
+
+    def shelves_use(v0):
+        trail = []
+        for _ in range(jax.lax.axis_size("pair")):
+            trail.append(v0)
+        return jnp.concatenate(jax.lax.all_to_all(jnp.stack(trail), "pair", 0, 0), 0)
+
     groups = lax.axis_size("dp")
     rows_here = embedding.shape[0]
     capacity = 2 * rows_here // groups
@@ -53,7 +60,7 @@
     best_seen = jnp.full((slot_count,), -1.0, jnp.float32)
     piece = (
         lax.all_gather(got_rows, "pair", axis=0, tiled=True),
-        lax.all_gather(got_labels, "pair", axis=0, tiled=True),
+        shelves_use(got_labels),
         lax.all_gather(got_order, "pair", axis=0, tiled=True),
     )
     piece_count = piece[0].shape[0]

time: 162 us -> 158 us (0.975)
  the two profiles are of different devices: /device:TPU:8 before, /device:TPU:1 now
where the time goes in v1:
time: 158 us; the launch traced here: 157 us
  blocking collectives  59.8 us (38%)
  waiting for transfers between devices  37.4 us (24%)
  starting transfers between devices  25.4 us (16%)
  between operations  13.5 us (9%)
  local copies, waits for them, and re-layouts  9.4 us (6%)
  other arithmetic  6.84 us (4%)
  matrix products  5.07 us (3%)
    all_to_all x1, blocking collectives, on_device(): lax.all_to_all(send_rows.reshape(groups, capacity, -1), 'dp', split_axis=...  48.9 us
    all_to_all x1, waiting for transfers between devices, on_device(): lax.all_to_all(best_seen.reshape(groups, capacity), 'dp', split_axis=0, c...  13.4 us
    all_to_all x1, waiting for transfers between devices, on_device(): lax.all_to_all(send_order.reshape(groups, capacity), 'dp', split_axis=0,...  12.2 us
    all_to_all x1, waiting for transfers between devices, on_device(): lax.all_to_all(send_labels.reshape(groups, capacity), 'dp', split_axis=0,...  11.8 us
    all_gather x1, blocking collectives, on_device(): lax.all_gather(got_order, 'pair', axis=0, tiled=True)  10.8 us
    all_to_all x1, starting transfers between devices, shelves_use(): jax.lax.all_to_all(jnp.stack(trail), 'pair', 0, 0)  8.41 us
    all_to_all x1, starting transfers between devices, on_device(): lax.all_to_all(send_labels.reshape(groups, capacity), 'dp', split_axis=0,...  7.86 us
    dot_general x4, matrix products, tile_best(): scores = jnp.dot(own_rows, other_rows.T, preferred_element_type=jnp.float32)  5.07 us
  transfers between devices with their start and end apart: 5, of which 3 were waited for; matrix products, arithmetic and copies ran while one was open for 3% of the time, Pallas kernels for 0%

profile of v1, /device:TPU:1, one launch (start us, length us, event | category | flops | bytes accessed | tf_op | source)
XLA Modules:
  0.0 157.5 jit_solution(15762520729891794870)
XLA Ops:
  6.5 0.7 and_select_fusion
  7.2 1.1 fusion.8
  8.4 0.2 reduce_window_sum.11
  8.7 0.7 compare_select_fusion
  9.4 1.8 %scatter_custom_fusion.2 = bf16[256,1024]{1,0:T(8,128)(2,1)S(1)} fusion(s32[128]{0:T(128)S(1)} %compare_select_fusion, bf16[128,1024]{1,0:T(8,128)(2,1)} %param.3, f32[128]{0:T(128)S(1)} %add_rsqrt_fusion, bf16[]{:T(256)} %constant.18.clone.1), kind=kCustom, calls=%fused_computation.20 | custom fusion | flops 393216 | bytes 786946 | tf_op jit(solution)/shard_map/scatter | solution.py:42
  11.2 0.2 reshape.129
  11.4 48.9 %all_to_all.35 = bf16[64,4,1024]{2,1,0:T(4,128)(2,1)S(1)} all-to-all(bf16[64,4,1024]{2,1,0:T(4,128)(2,1)S(1)} %reshape.129), channel_id=1, replica_groups=mesh['dp'=64,'pair'=8] {'dp'}, dimensions={0} | all-to-all | bytes 1048576 | tf_op jit(solution)/shard_map/all_to_all | solution.py:47
  60.3 0.9 reshape.130
  61.3 1.2 scatter_custom_fusion
  62.5 0.7 all_to_all.23
  63.2 7.9 %all-to-all-start = ((s32[64,1,4]{2,1,0:T(1,128)}), s32[64,1,4]{2,1,0:T(1,128)S(1)}, u32[]{:S(2)}, u32[]{:S(2)}) async-start(s32[64,1,4]{2,1,0:T(1,128)} %bitcast), calls=%async_computation | async-start | bytes 65536 | tf_op jit(solution)/shard_map/all_to_all | solution.py:50
  71.1 1.1 scatter_custom_fusion.1
  72.2 0.7 all_to_all.26
  72.9 11.8 %all-to-all-done = s32[64,1,4]{2,1,0:T(1,128)S(1)} async-done(((s32[64,1,4]{2,1,0:T(1,128)}), s32[64,1,4]{2,1,0:T(1,128)S(1)}, u32[]{:S(2)}, u32[]{:S(2)}) %all-to-all-start) | async-done | bytes 1056 | tf_op jit(solution)/shard_map/all_to_all | solution.py:50
  84.7 4.5 %all-to-all-start.2 = ((s32[64,1,4]{2,1,0:T(1,128)}), s32[64,1,4]{2,1,0:T(1,128)S(1)}, u32[]{:S(2)}, u32[]{:S(2)}) async-start(s32[64,1,4]{2,1,0:T(1,128)} %bitcast.2), calls=%async_computation.2 | async-start | bytes 65536 | tf_op jit(solution)/shard_map/all_to_all | solution.py:53
  89.2 0.5 broadcast.72
  89.7 0.7 reduce.12
  90.6 12.2 %all-to-all-done.2 = s32[64,1,4]{2,1,0:T(1,128)S(1)} async-done(((s32[64,1,4]{2,1,0:T(1,128)}), s32[64,1,4]{2,1,0:T(1,128)S(1)}, u32[]{:S(2)}, u32[]{:S(2)}) %all-to-all-start.2) | async-done | bytes 1056 | tf_op jit(solution)/shard_map/all_to_all | solution.py:53
  102.8 0.6 stack.6
  103.4 8.4 %all-to-all-start.1 = ((s32[8,1,256]{2,1,0:T(1,128)}), s32[8,1,256]{2,1,0:T(1,128)S(1)}, u32[]{:S(2)}, u32[]{:S(2)}) async-start(s32[8,1,256]{2,1,0:T(1,128)} %stack.6), calls=%async_computation.1 | async-start | bytes 16384 | tf_op jit(solution)/shard_map/all_to_all | solution.py:25
  111.8 0.7 reduce.11
  112.6 10.8 %all-gather = s32[8,1,256]{2,1,0:T(1,128)S(1)} all-gather(s32[1,1,256]{2,1,0:T(1,128)S(1)} %reshape.168), channel_id=1, replica_groups=mesh['dp'=64,'pair'=8] {'pair'}, dimensions={0}, use_global_device_ids=true | all-gather | bytes 9216 | tf_op jit(solution)/shard_map/all_gather | solution.py:64
  123.7 2.1 %fusion.3 = f32[256]{0:T(256)S(1)} fusion(bf16[256,1024]{1,0:T(8,128)(2,1)} %reshape.130, bf16[2048,1024]{1,0:T(8,128)(2,1)} %all-gather.3.cloned.1.call-done, s32[512]{0:T(512)S(1)} %bitcast.23, s32[512]{0:T(512)S(1)} %bitcast.27, pred[256]{0:T(512)(128)(4,1)S(1)} %broadcast_compare_fusion, s32[256]{0:T(256)S(1)} %reshape.128, s32[256]{0:T(256)S(1)} %stack.5), kind=kOutput, calls=%fused_computation.11 | convolution fusion | flops 269221632 | bytes 1580288 | tf_op jit(solution)/shard_map/dot_general | solution.py:10
  125.8 1.8 %fusion.2 = f32[256]{0:T(256)S(1)} fusion(bf16[256,1024]{1,0:T(8,128)(2,1)S(1)} %copy-done, bf16[2048,1024]{1,0:T(8,128)(2,1)} %all-gather.3.cloned.1.call-done, s32[512]{0:T(512)S(1)} %bitcast.22, s32[512]{0:T(512)S(1)} %bitcast.26, pred[256]{0:T(512)(128)(4,1)S(1)} %broadcast_compare_fusion, s32[256]{0:T(256)S(1)} %reshape.128, s32[256]{0:T(256)S(1)} %stack.5), kind=kOutput, calls=%fused_computation.10 | convolution fusion | flops 269221632 | bytes 1580288 | tf_op jit(solution)/shard_map/dot_general | solution.py:10
  127.6 0.6 fusion.1
  128.2 0.6 fusion
  128.7 0.7 max.41
  129.5 4.6 %all-to-all-start.4 = ((f32[64,1,4]{2,1,0:T(1,128)}), f32[64,1,4]{2,1,0:T(1,128)S(1)}, u32[]{:S(2)}, u32[]{:S(2)}) async-start(f32[64,1,4]{2,1,0:T(1,128)} %bitcast.10), calls=%async_computation.4 | async-start | bytes 65536 | tf_op jit(solution)/shard_map/all_to_all | solution.py:78
  134.1 13.4 %all-to-all-done.4 = f32[64,1,4]{2,1,0:T(1,128)S(1)} async-done(((f32[64,1,4]{2,1,0:T(1,128)}), f32[64,1,4]{2,1,0:T(1,128)S(1)}, u32[]{:S(2)}, u32[]{:S(2)}) %all-to-all-start.4) | async-done | bytes 1056 | tf_op jit(solution)/shard_map/all_to_all | solution.py:78
  147.5 0.5 broadcast.74
  148.0 0.7 reduce.13
  148.8 1.8 %gather_fusion = f32[128]{0:T(128)} fusion(f32[256]{0:T(256)S(1)} %reshape.131, s32[1024]{0:T(1024)S(1)} %pad_clamp_fusion), kind=kCustom, calls=%fused_computation | custom fusion | bytes 1536 | tf_op jit(solution)/shard_map/gather | solution.py:81
  (20 shorter events, 0.8 us)
Async XLA Ops:
  6.5 117.1 %all-gather.3.cloned.1.call-start = ((), (), s32[]{:S(2)}) async-start(), calls=%async_computation.5 | async-start | bytes 4718592 | tf_op jit(solution)/shard_map/all_gather | solution.py:62
  61.3 64.5 %copy-start = (bf16[256,1024]{1,0:T(8,128)(2,1)S(1)}, bf16[256,1024]{1,0:T(8,128)(2,1)}, u32[]{:S(2)}) copy-start(bf16[256,1024]{1,0:T(8,128)(2,1)} %reshape.130) | copy-start | bytes 1572868
  63.2 21.5 %all-to-all-start = ((s32[64,1,4]{2,1,0:T(1,128)}), s32[64,1,4]{2,1,0:T(1,128)S(1)}, u32[]{:S(2)}, u32[]{:S(2)}) async-start(s32[64,1,4]{2,1,0:T(1,128)} %bitcast), calls=%async_computation | async-start | bytes 65536 | tf_op jit(solution)/shard_map/all_to_all | solution.py:50
  84.7 18.1 %all-to-all-start.2 = ((s32[64,1,4]{2,1,0:T(1,128)}), s32[64,1,4]{2,1,0:T(1,128)S(1)}, u32[]{:S(2)}, u32[]{:S(2)}) async-start(s32[64,1,4]{2,1,0:T(1,128)} %bitcast.2), calls=%async_computation.2 | async-start | bytes 65536 | tf_op jit(solution)/shard_map/all_to_all | solution.py:53
  103.4 20.2 %all-to-all-start.1 = ((s32[8,1,256]{2,1,0:T(1,128)}), s32[8,1,256]{2,1,0:T(1,128)S(1)}, u32[]{:S(2)}, u32[]{:S(2)}) async-start(s32[8,1,256]{2,1,0:T(1,128)} %stack.6), calls=%async_computation.1 | async-start | bytes 16384 | tf_op jit(solution)/shard_map/all_to_all | solution.py:25
  123.6 3.9 %copy-start.1 = (bf16[2048,1024]{1,0:T(8,128)(2,1)S(1)}, bf16[2048,1024]{1,0:T(8,128)(2,1)}, u32[]{:S(2)}) copy-start(bf16[2048,1024]{1,0:T(8,128)(2,1)} %all-gather.3.cloned.1.call-done) | copy-start | bytes 12582916
  129.5 18.0 %all-to-all-start.4 = ((f32[64,1,4]{2,1,0:T(1,128)}), f32[64,1,4]{2,1,0:T(1,128)S(1)}, u32[]{:S(2)}, u32[]{:S(2)}) async-start(f32[64,1,4]{2,1,0:T(1,128)} %bitcast.10), calls=%async_computation.4 | async-start | bytes 65536 | tf_op jit(solution)/shard_map/all_to_all | solution.py:78
Sparse Core Ops, SparseCore 0:
  61.4 35.0 all-gather.2
